TPU v7x, 256 devices: a whole 4x4x8 slice. The times are simulated.
256 devices in a mesh: row: 4 (over z_lo), col: 64 (over y, x, z_hi, core).
Axes of the slice: x: 4, y: 4, z: 8 (z_hi: 2, z_lo: 4; z = z_hi * 4 + z_lo), core: 2. Of those that a mesh axis runs over, the one named last changes fastest.
Arguments:
- iterate: float32 [256, 131072], P('row', 'col'), may hold values from -6 to 6
- residual: float32 [256, 131072], P('row', 'col'), may hold values from -24 to 24
- direction: float32 [256, 131072], P('row', 'col'), may hold values from -24 to 24
- window_weight: float32 [16, 8192], P('row', 'col'), may hold values from 0.2 to 5
- freq_weight: float32 [32, 32], replicated, may hold values from 0.2 to 5
Outputs:
- new_iterate: float32 [256, 131072], P('row', 'col')
- new_residual: float32 [256, 131072], P('row', 'col')
- new_direction: float32 [256, 131072], P('row', 'col')
All inputs are finite; a program needn't handle non-finite values.
Results may differ from a plain program's by a relative error of at most 0.0003.
Values sent between devices are 32-bit elements; how exact they have to be, the bound alone decides.
No kernel may reach another device: no remote copies, remote signals or barrier semaphores. Data moves between devices by JAX's collectives and lax.ppermute only.
A program may use at most 64 MiB of HBM per device.

v0:
```python
import jax
import jax.numpy as jnp
from jax import lax
from jax.sharding import Mesh
from jax.sharding import PartitionSpec as P

COL = ("col_0", "col_1", "col_2", "col_3")
ROW_COL = ("row", "col_0", "col_1", "col_2", "col_3")
precise = lax.Precision.HIGHEST
damping = 0.5


def passed_along(value, axis, steps):
    count = lax.axis_size(axis)
    leading, last = (max(0, -steps), min(count, count - steps))
    return lax.ppermute(value, axis, [(source, source + steps) for source in range(leading, last)])


def over_axes(x, axes):
    for axis in axes:
        x = lax.psum(x, axis)
    return x


def tables():
    positions = jnp.arange(32, dtype=jnp.float32)
    window = jnp.exp(-0.5 * ((positions - 15.5) / 8.0) ** 2)
    phases = 2.0 * jnp.pi * jnp.outer(positions, positions) / 32.0
    cos_part = jnp.cos(phases) * window[None, :] / jnp.sqrt(32.0)
    sin_part = -jnp.sin(phases) * window[None, :] / jnp.sqrt(32.0)
    column_table = jnp.concatenate([cos_part.T, sin_part.T], axis=1)
    cos_split = cos_part.reshape(32, 2, 16)
    sin_split = sin_part.reshape(32, 2, 16)
    upper = jnp.stack([cos_split, -sin_split], axis=-1)
    lower = jnp.stack([sin_split, cos_split], axis=-1)
    row_table = jnp.concatenate([upper, lower], axis=0).reshape(64, 64)
    return (column_table, row_table)


def analyze(region, column_table, row_table):
    win_rows = region.shape[0] // 16 - 1
    win_cols = region.shape[1] // 16 - 1
    blocks = region.reshape(win_rows + 1, 16, win_cols + 1, 16)
    section_one = jnp.einsum(
        "akbl,lp->akpb", blocks[:, :, :win_cols], column_table[:16], precision=precise
    )
    section_one = section_one + jnp.einsum(
        "akbl,lp->akpb", blocks[:, :, 1:], column_table[16:], precision=precise
    )
    section_one = section_one.reshape(win_rows + 1, 16, 2, 32, win_cols)
    paired = jnp.stack([section_one[:-1], section_one[1:]], axis=1).reshape(
        win_rows, 64, 32, win_cols
    )
    return jnp.einsum("tm,amvb->atvb", row_table, paired, precision=precise)


def weigh(coefficients, window_weight, freq_weight):
    doubled = jnp.concatenate([freq_weight, freq_weight], axis=0)
    return coefficients * doubled[None, :, :, None] * window_weight[:, None, None, :]


def synthesize(coefficients, column_table, row_table):
    win_rows = coefficients.shape[0]
    win_cols = coefficients.shape[3]
    spread = jnp.einsum("tm,atvb->amvb", row_table, coefficients, precision=precise)
    spread = spread.reshape(win_rows, 2, 16, 64, win_cols)
    stacked = jnp.pad(spread[:, 0], ((0, 1), (0, 0), (0, 0), (0, 0))) + jnp.pad(
        spread[:, 1], ((1, 0), (0, 0), (0, 0), (0, 0))
    )
    lower_piece = jnp.einsum("akpb,lp->akbl", stacked, column_table[:16], precision=precise)
    upper_piece = jnp.einsum("akpb,lp->akbl", stacked, column_table[16:], precision=precise)
    blocks = jnp.pad(lower_piece, ((0, 0), (0, 0), (0, 1), (0, 0))) + jnp.pad(
        upper_piece, ((0, 0), (0, 0), (1, 0), (0, 0))
    )
    return blocks.reshape(16 * (win_rows + 1), 16 * (win_cols + 1))


def per_device(iterate, residual, direction, window_weight, freq_weight):
    column_table, row_table = tables()
    height, breadth = direction.shape
    beside = passed_along(direction[:, :16], COL, -1)
    widened = jnp.concatenate([direction, beside], axis=1)
    below = passed_along(widened[:16], "row", -1)
    region = jnp.concatenate([widened, below], axis=0)
    coefficients = weigh(analyze(region, column_table, row_table), window_weight, freq_weight)
    spread = synthesize(coefficients, column_table, row_table)
    arrived_rows = passed_along(spread[height:], "row", 1)
    upper_rows = jnp.concatenate([spread[:16] + arrived_rows, spread[16:height]], axis=0)
    arrived_cols = passed_along(upper_rows[:, breadth:], COL, 1)
    synthesized = jnp.concatenate(
        [upper_rows[:, :16] + arrived_cols, upper_rows[:, 16:breadth]], axis=1
    )
    applied = synthesized + damping * direction
    norm_now, curvature, cross_term, image_norm = (
        over_axes(jnp.sum(residual * residual), ROW_COL),
        over_axes(jnp.sum(direction * applied), ROW_COL),
        over_axes(jnp.sum(residual * applied), ROW_COL),
        over_axes(jnp.sum(applied * applied), ROW_COL),
    )
    step_length = norm_now / curvature
    new_iterate = iterate + step_length * direction
    new_residual = residual - step_length * applied
    norm_next = norm_now - 2.0 * step_length * cross_term + step_length * step_length * image_norm
    new_direction = new_residual + norm_next / norm_now * direction
    return (new_iterate, new_residual, new_direction)


def solution(mesh):
    finer = Mesh(
        mesh.devices.reshape(mesh.shape["row"], 4, 4, 2, 2),
        ("row", "col_0", "col_1", "col_2", "col_3"),
    )
    return jax.shard_map(
        per_device,
        mesh=finer,
        in_specs=(P("row", COL), P("row", COL), P("row", COL), P("row", COL), P()),
        out_specs=(P("row", COL), P("row", COL), P("row", COL)),
        check_vma=False,
    )
```

profile of v0, /device:TPU:1, one launch (start us, length us, event | category | flops | bytes accessed | tf_op | source)
XLA Modules:
  0.0 132.1 jit_solution(15178026938067578234)
XLA Ops:
  0.6 0.8 slice.62
  1.4 5.1 %collective-permute-start = (f32[64,16]{1,0:T(8,128)S(1)}, f32[64,16]{1,0:T(8,128)S(1)}, u32[]{:S(2)}, u32[]{:S(2)}) collective-permute-start(f32[64,16]{1,0:T(8,128)S(1)} %slice.62), channel_id=1, source_target_pairs={{1,0},{2,1},{3,2},{4,3},{5,4},{6,5},{7,6},{8,7},{9,8},{10,9},{11,1... | collective-permute-start | bytes 12296 | tf_op jit(solution)/shard_map/ppermute | solution.py:16
  6.6 1.1 constant_dynamic-update-slice_fusion.1
  7.7 0.1 multiply_multiply_fusion.4
  7.7 0.1 fusion.26
  7.9 0.8 pad_maximum_fusion.2
  8.7 4.5 %collective-permute-done = f32[64,16]{1,0:T(8,128)S(1)} collective-permute-done((f32[64,16]{1,0:T(8,128)S(1)}, f32[64,16]{1,0:T(8,128)S(1)}, u32[]{:S(2)}, u32[]{:S(2)}) %collective-permute-start) | collective-permute-done | bytes 4128 | tf_op jit(solution)/shard_map/ppermute | solution.py:16
  13.2 1.3 collective-permute-start.1
  14.5 0.1 maximum_maximum_fusion
  14.6 0.1 copy.31
  14.7 0.1 fusion.25
  14.7 4.3 %collective-permute-done.1 = f32[16,2064]{1,0:T(8,128)S(1)} collective-permute-done((f32[16,2064]{1,0:T(8,128)S(1)}, f32[16,2064]{1,0:T(8,128)S(1)}, u32[]{:S(2)}, u32[]{:S(2)}) %collective-permute-start.1) | collective-permute-done | bytes 132128 | tf_op jit(solution)/shard_map/ppermute | solution.py:16
  19.0 3.2 %reshape.132 = f32[5,16,129,16]{3,2,1,0:T(8,128)} reshape(f32[80,2064]{1,0:T(8,128)S(1)} %pad_maximum_fusion) | data formatting | bytes 1320960 | tf_op jit(solution)/shard_map/reshape | solution.py:43
  22.3 0.0 copy-start
  22.3 8.1 %fusion = f32[64,5,16,128]{3,0,2,1:T(8,128)S(1)} fusion(f32[16,64,1,1]{1,0,3,2:T(8,128)S(1)} %fusion.25, f32[5,16,129,16]{3,2,1,0:T(8,128)} %reshape.132), kind=kOutput, calls=%fused_computation | convolution fusion | flops 125829120 | bytes 7868416 | tf_op jit(solution)/shard_map/akbl,lp->akpb/dot_general | solution.py:47
  30.4 0.0 copy-done
  30.4 5.8 %add_bitcast_fusion = f32[5,16,64,128]{3,2,1,0:T(8,128)S(1)} fusion(f32[64,5,16,128]{3,0,2,1:T(8,128)S(1)} %fusion, f32[5,16,129,16]{3,2,1,0:T(8,128)S(1)} %copy-done, f32[32,32]{1,0:T(8,128)S(1)} %get-tuple-element.40, f32[32,32]{1,0:T(8,128)S(1)} %get-tuple-element.41), kind=kOutput, calls=%fused_computation.12 | convolution fusion | flops 126485504 | bytes 10518528 | tf_op jit(solution)/shard_map/akbl,lp->akpb/dot_general | solution.py:44
  36.2 0.6 fusion.35
  36.8 1.2 copy.29
  38.1 1.2 copy.30
  39.3 0.0 copy-start.4
  39.3 4.2 %fusion.4 = f32[4,32,128,64,1,1]{2,3,5,4,1,0:T(8,128)S(1)} fusion(f32[4,1,16,2,32,128]{5,2,3,1,4,0:T(8,128)S(1)} %copy.30, f32[4,1,16,2,32,128]{5,2,3,1,4,0:T(8,128)S(1)} %copy.29, f32[64,2,16,2]{0,2,3,1:T(8,128)S(1)} %maximum_maximum_fusion), kind=kOutput, calls=%fused_computation.4 | convolution fusion | flops 806354944 | bytes 8404992 | tf_op jit(solution)/shard_map/tm,amvb->atvb/dot_general | solution.py:54
  43.5 0.0 copy-done.4
  43.5 4.4 %fusion.11 = f32[4,64,32,128]{3,1,2,0:T(8,128)S(1)} fusion(f32[64,64,1,1]{0,1,3,2:T(8,128)S(1)} %bitcast.50, f32[4,32,128,64,1,1]{2,3,5,4,1,0:T(8,128)S(1)} %fusion.4, f32[4,128]{1,0:T(4,128)S(1)} %copy-done.4, f32[64,32]{0,1:T(8,128)S(1)} %copy.31), kind=kOutput, calls=%fused_computation.13 | convolution fusion | flops 807403520 | bytes 8415232 | tf_op jit(solution)/shard_map/tm,atvb->amvb/dot_general | solution.py:65
  47.9 2.4 %copy.33 = f32[4,64,32,128]{3,2,1,0:T(8,128)S(1)} copy(f32[4,64,32,128]{3,1,2,0:T(8,128)S(1)} %fusion.11) | data formatting | bytes 8388608 | tf_op jit(solution)/shard_map/tm,atvb->amvb/transpose | solution.py:65
  50.3 0.6 slice_bitcast_fusion.1
  50.9 1.5 %fusion.19 = f32[5,16,128,16]{2,3,1,0:T(8,128)S(1)} fusion(f32[4,16,64,128]{3,2,1,0:T(8,128)S(1)} %get-tuple-element.31, f32[4,16,64,128]{3,2,1,0:T(8,128)S(1)} %get-tuple-element.30, f32[32,32]{1,0:T(8,128)S(1)} %get-tuple-element.40, f32[32,32]{1,0:T(8,128)S(1)} %get-tuple-element.41), kind=kOutput, calls=%fused_computation.19 | convolution fusion | flops 126485504 | bytes 4857856 | tf_op jit(solution)/shard_map/akpb,lp->akbl/dot_general | solution.py:70
  52.4 1.5 %fusion.18 = f32[5,16,128,16]{2,3,1,0:T(8,128)S(1)} fusion(f32[16,64,1,1]{1,0,3,2:T(8,128)S(1)} %fusion.25, f32[4,16,64,128]{3,2,1,0:T(8,128)S(1)} %get-tuple-element.31, f32[4,16,64,128]{3,2,1,0:T(8,128)S(1)} %get-tuple-element.30), kind=kOutput, calls=%fused_computation.18 | convolution fusion | flops 126484480 | bytes 4853760 | tf_op jit(solution)/shard_map/akpb,lp->akbl/dot_general | solution.py:71
  53.9 0.2 pad_add_fusion.4
  54.1 0.4 copy.36
  54.5 1.0 slice.74
  55.5 3.4 %collective-permute-start.2 = (f32[16,2064]{1,0:T(8,128)}, f32[16,2064]{1,0:T(8,128)}, u32[]{:S(2)}, u32[]{:S(2)}) collective-permute-start(f32[16,2064]{1,0:T(8,128)} %slice.74), channel_id=1, source_target_pairs={{0,64},{64,128},{128,192},{1,65},{65,129},{129,193},{2,66},{66,130... | collective-permute-start | bytes 396296 | tf_op jit(solution)/shard_map/ppermute | solution.py:16
  58.9 0.4 copy.35
  59.3 0.3 slice.72
  59.6 1.1 pad_add_fusion.3
  60.7 2.1 %copy.37 = f32[3,16,129,16]{3,2,1,0:T(8,128)S(1)} copy(f32[3,16,129,16]{2,3,1,0:T(8,128)} %pad_add_fusion.3) | data formatting | bytes 792576 | tf_op jit(solution)/shard_map/slice | solution.py:88
  62.8 1.6 %slice.76 = f32[48,2064]{1,0:T(8,128)} reshape(f32[3,16,129,16]{3,2,1,0:T(8,128)S(1)} %copy.37) | data formatting | bytes 792576 | tf_op jit(solution)/shard_map/slice | solution.py:88
  64.4 0.0 copy-start.1
  64.4 0.0 copy-start.2
  64.4 0.0 copy-start.3
  64.5 0.0 collective-permute-done.2
  64.5 1.0 add.98
  65.5 0.7 pad_maximum_fusion.1
  66.2 3.8 %collective-permute-start.3 = (f32[64,16]{1,0:T(8,128)S(1)}, f32[64,16]{1,0:T(8,128)S(1)}, u32[]{:S(2)}, u32[]{:S(2)}) collective-permute-start(f32[64,16]{1,0:T(8,128)S(1)} %pad_maximum_fusion.1), channel_id=1, source_target_pairs={{0,1},{1,2},{2,3},{3,4},{4,5},{5,6},{6,7},{7,8},{8,9},{9,10},{10,1... | collective-permute-start | bytes 12296 | tf_op jit(solution)/shard_map/ppermute | solution.py:16
  70.1 1.0 collective-permute-done.3
  71.1 0.7 maximum_add_fusion
  71.8 2.1 %multiply_reduce_fusion = (f32[]{:T(128)}, f32[]{:T(128)}, f32[]{:T(128)}, f32[]{:T(128)}, f32[64,2048]{1,0:T(8,128)S(1)}) fusion(f32[64,2048]{1,0:T(8,128)} %param.6, f32[64,2048]{1,0:T(8,128)} %param.7, f32[48,2064]{1,0:T(8,128)} %slice.76, f32[16,2064]{1,0:T(8,128)S(1)} %add.98, f32[64,16]{1,0:T(8,128)S(1)} %maximum_add_fusion), kind=kLoop, calls=%fused_computation.27 | loop fusion | flops 1966076 | bytes 2105360 | tf_op jit(solution)/shard_map/reduce_sum | solution.py:98
  73.9 7.4 %all-reduce.6 = (f32[]{:T(128)}, f32[]{:T(128)}, f32[]{:T(128)}, f32[]{:T(128)}) all-reduce(f32[]{:T(128)} %get-tuple-element.5, f32[]{:T(128)} %get-tuple-element.6, f32[]{:T(128)} %get-tuple-element.4, f32[]{:T(128)} %get-tuple-element.3), channel_id=1, replica_groups=mesh['row'=4,'col_0'=4,'col_1'=4,'col_2'=2,'col_3'=2] {'row'}, use_global_device_ids=true, to_apply=%region_1.2 | all-reduce | flops 4 | bytes 32 | tf_op jit(solution)/shard_map/psum | solution.py:21
  81.3 11.2 %all-reduce.5 = (f32[]{:T(128)}, f32[]{:T(128)}, f32[]{:T(128)}, f32[]{:T(128)}) all-reduce(f32[]{:T(128)} %get-tuple-element.15, f32[]{:T(128)} %get-tuple-element.16, f32[]{:T(128)} %get-tuple-element.17, f32[]{:T(128)} %get-tuple-element.18), channel_id=1, replica_groups=mesh['row'=4,'col_0'=4,'col_1'=4,'col_2'=2,'col_3'=2] {'col_0'}, use_global_device_ids=true, to_apply=%region_2.3 | all-reduce | flops 4 | bytes 32 | tf_op jit(solution)/shard_map/psum | solution.py:21
  92.6 8.9 %all-reduce.4 = (f32[]{:T(128)}, f32[]{:T(128)}, f32[]{:T(128)}, f32[]{:T(128)}) all-reduce(f32[]{:T(128)} %get-tuple-element.11, f32[]{:T(128)} %get-tuple-element.12, f32[]{:T(128)} %get-tuple-element.13, f32[]{:T(128)} %get-tuple-element.14), channel_id=1, replica_groups=mesh['row'=4,'col_0'=4,'col_1'=4,'col_2'=2,'col_3'=2] {'col_1'}, use_global_device_ids=true, to_apply=%region_3.4 | all-reduce | flops 4 | bytes 32 | tf_op jit(solution)/shard_map/psum | solution.py:21
  101.5 8.3 %all-reduce.8 = (f32[]{:T(128)}, f32[]{:T(128)}, f32[]{:T(128)}, f32[]{:T(128)}) all-reduce(f32[]{:T(128)} %get-tuple-element.7, f32[]{:T(128)} %get-tuple-element.8, f32[]{:T(128)} %get-tuple-element.9, f32[]{:T(128)} %get-tuple-element.10), channel_id=1, replica_groups=mesh['row'=4,'col_0'=4,'col_1'=4,'col_2'=2,'col_3'=2] {'col_2'}, use_global_device_ids=true, to_apply=%region_4.5 | all-reduce | flops 4 | bytes 32 | tf_op jit(solution)/shard_map/psum | solution.py:21
  109.8 17.1 %all-reduce.7 = (f32[]{:T(128)}, f32[]{:T(128)}, f32[]{:T(128)}, f32[]{:T(128)}) all-reduce(f32[]{:T(128)} %get-tuple-element.23, f32[]{:T(128)} %get-tuple-element.24, f32[]{:T(128)} %get-tuple-element.25, f32[]{:T(128)} %get-tuple-element.26), channel_id=1, replica_groups=mesh['row'=4,'col_0'=4,'col_1'=4,'col_2'=2,'col_3'=2] {'col_3'}, use_global_device_ids=true, to_apply=%region_5.6 | all-reduce | flops 4 | bytes 32 | tf_op jit(solution)/shard_map/psum | solution.py:21
  130.9 0.0 copy-done.1
  130.9 0.0 copy-done.2
  130.9 0.0 copy-done.3
  130.9 1.2 multiply_add_fusion
  (6 shorter events, 0.1 us)
Async XLA Ops:
  1.4 11.8 %collective-permute-start = (f32[64,16]{1,0:T(8,128)S(1)}, f32[64,16]{1,0:T(8,128)S(1)}, u32[]{:S(2)}, u32[]{:S(2)}) collective-permute-start(f32[64,16]{1,0:T(8,128)S(1)} %slice.62), channel_id=1, source_target_pairs={{1,0},{2,1},{3,2},{4,3},{5,4},{6,5},{7,6},{8,7},{9,8},{10,9},{11,1... | collective-permute-start | bytes 12296 | tf_op jit(solution)/shard_map/ppermute | solution.py:16
  13.2 5.8 %collective-permute-start.1 = (f32[16,2064]{1,0:T(8,128)S(1)}, f32[16,2064]{1,0:T(8,128)S(1)}, u32[]{:S(2)}, u32[]{:S(2)}) collective-permute-start(f32[16,2064]{1,0:T(8,128)S(1)} %slice.82), channel_id=1, source_target_pairs={{64,0},{128,64},{192,128},{65,1},{129,65},{193,129},{66,2},{130,66... | collective-permute-start | bytes 396296 | tf_op jit(solution)/shard_map/ppermute | solution.py:16
  22.3 8.1 %copy-start = (f32[5,16,129,16]{3,2,1,0:T(8,128)S(1)}, f32[5,16,129,16]{3,2,1,0:T(8,128)}, u32[]{:S(2)}) copy-start(f32[5,16,129,16]{3,2,1,0:T(8,128)} %reshape.132) | copy-start | bytes 1981444
  39.3 4.2 %copy-start.4 = (f32[4,128]{1,0:T(4,128)S(1)}, f32[4,128]{1,0:T(4,128)}, u32[]{:S(2)}) copy-start(f32[4,128]{1,0:T(4,128)} %param.8) | copy-start | bytes 6148
  55.5 8.9 %collective-permute-start.2 = (f32[16,2064]{1,0:T(8,128)}, f32[16,2064]{1,0:T(8,128)}, u32[]{:S(2)}, u32[]{:S(2)}) collective-permute-start(f32[16,2064]{1,0:T(8,128)} %slice.74), channel_id=1, source_target_pairs={{0,64},{64,128},{128,192},{1,65},{65,129},{129,193},{2,66},{66,130... | collective-permute-start | bytes 396296 | tf_op jit(solution)/shard_map/ppermute | solution.py:16
  64.4 66.4 %copy-start.1 = (f32[64,2048]{1,0:T(8,128)S(1)}, f32[64,2048]{1,0:T(8,128)}, u32[]{:S(2)}) copy-start(f32[64,2048]{1,0:T(8,128)} %param.7) | copy-start | bytes 1572868
  64.4 66.4 %copy-start.2 = (f32[64,2048]{1,0:T(8,128)S(1)}, f32[64,2048]{1,0:T(8,128)}, u32[]{:S(2)}) copy-start(f32[64,2048]{1,0:T(8,128)} %param.6) | copy-start | bytes 1572868
  64.4 66.5 %copy-start.3 = (f32[64,2048]{1,0:T(8,128)S(1)}, f32[64,2048]{1,0:T(8,128)}, u32[]{:S(2)}) copy-start(f32[64,2048]{1,0:T(8,128)} %param.5) | copy-start | bytes 1572868
  66.2 4.8 %collective-permute-start.3 = (f32[64,16]{1,0:T(8,128)S(1)}, f32[64,16]{1,0:T(8,128)S(1)}, u32[]{:S(2)}, u32[]{:S(2)}) collective-permute-start(f32[64,16]{1,0:T(8,128)S(1)} %pad_maximum_fusion.1), channel_id=1, source_target_pairs={{0,1},{1,2},{2,3},{3,4},{4,5},{5,6},{6,7},{7,8},{8,9},{9,10},{10,1... | collective-permute-start | bytes 12296 | tf_op jit(solution)/shard_map/ppermute | solution.py:16
where the time goes:
time: 133 us; the launch traced here: 132 us
  blocking collectives  52.9 us (40%)
  matrix products  25.5 us (19%)
  local copies, waits for them, and re-layouts  17 us (13%)
  starting transfers between devices  13.6 us (10%)
  waiting for transfers between devices  9.75 us (7%)
  other arithmetic  8.5 us (6%)
  between operations  4.85 us (4%)
    psum x5, blocking collectives, over_axes(): x = lax.psum(x, axis)  52.9 us
    ppermute x4, starting transfers between devices, passed_along(): lax.ppermute(value, axis, [(source, source + steps) for source in range(l...  13.6 us
    ppermute x4, waiting for transfers between devices, passed_along(): lax.ppermute(value, axis, [(source, source + steps) for source in range(l...  9.75 us
    dot_general x1, matrix products, analyze(): jnp.einsum('akbl,lp->akpb', blocks[:, :, 1:], column_table[16:], precisio...  8.08 us
    dot_general x1, matrix products, analyze(): jnp.einsum('akbl,lp->akpb', blocks[:, :, :win_cols], column_table[:16], p...  5.81 us
    dot_general x1, matrix products, synthesize(): jnp.einsum('tm,atvb->amvb', row_table, coefficients, precision=precise)  4.37 us
    dot_general x1, matrix products, analyze(): return jnp.einsum('tm,amvb->atvb', row_table, paired, precision=precise)  4.16 us
    slice x2, local copies, waits for them, and re-layouts, per_device(): spread[16:height]  3.69 us
  transfers between devices with their start and end apart: 4, of which 3 were waited for; matrix products, arithmetic and copies ran while one was open for 6% of the time, Pallas kernels for 0%

commit v1 on v0

--- a/solution.py
+++ b/solution.py
@@ -18,7 +18,7 @@
 
 def over_axes(x, axes):
     for axis in axes:
-        x = lax.psum(x, axis)
+        x = jnp.sum(lax.all_gather(x, axis), axis=0)
     return x
 
 

time: 133 us -> 172 us (1.29)
  local copies, waits for them, and re-layouts: 17 us -> 48.1 us
  other arithmetic: 8.5 us -> 20.5 us
  blocking collectives: 52.9 us -> 49.5 us
    psum x5 -> x0, blocking collectives: 52.9 us -> none  [over_axes(): x = lax.psum(x, axis)]
    unnamed x0 -> x5, blocking collectives: none -> 49.5 us
    unnamed x11 -> x66, local copies, waits for them, and re-layouts: 1.1 us -> 32.3 us
    reduce_sum x0 -> x20, other arithmetic: none -> 12 us  [over_axes(): x = jnp.sum(lax.all_gather(x, axis), axis=0)]
  transfers between devices with their start and end apart: 4 -> 4, of which waited for: 3 -> 3; matrix products, arithmetic and copies ran while one was open for 6% -> 5% of each run, Pallas kernels for 0% -> 0%
where the time goes in v1:
time: 172 us; the launch traced here: 171 us
  blocking collectives  49.5 us (29%)
  local copies, waits for them, and re-layouts  48.1 us (28%)
  matrix products  25.5 us (15%)
  other arithmetic  20.5 us (12%)
  starting transfers between devices  13.6 us (8%)
  waiting for transfers between devices  9.07 us (5%)
  between operations  4.91 us (3%)
    unnamed x5, blocking collectives  49.5 us
    unnamed x66, local copies, waits for them, and re-layouts  32.3 us
    ppermute x4, starting transfers between devices, passed_along(): lax.ppermute(value, axis, [(source, source + steps) for source in range(l...  13.6 us
    reduce_sum x20, other arithmetic, over_axes(): x = jnp.sum(lax.all_gather(x, axis), axis=0)  12 us
    ppermute x4, waiting for transfers between devices, passed_along(): lax.ppermute(value, axis, [(source, source + steps) for source in range(l...  9.07 us
    dot_general x1, matrix products, analyze(): jnp.einsum('akbl,lp->akpb', blocks[:, :, 1:], column_table[16:], precisio...  8.1 us
    dot_general x1, matrix products, analyze(): jnp.einsum('akbl,lp->akpb', blocks[:, :, :win_cols], column_table[:16], p...  5.8 us
    dot_general x1, matrix products, synthesize(): jnp.einsum('tm,atvb->amvb', row_table, coefficients, precision=precise)  4.38 us
  transfers between devices with their start and end apart: 4, of which 3 were waited for; matrix products, arithmetic and copies ran while one was open for 5% of the time, Pallas kernels for 0%

profile of v1, /device:TPU:1, one launch (start us, length us, event | category | flops | bytes accessed | tf_op | source)
XLA Modules:
  0.0 171.3 jit_solution(4003012283849033373)
XLA Ops:
  0.6 0.8 slice.62
  1.4 5.1 %collective-permute-start = (f32[64,16]{1,0:T(8,128)S(1)}, f32[64,16]{1,0:T(8,128)S(1)}, u32[]{:S(2)}, u32[]{:S(2)}) collective-permute-start(f32[64,16]{1,0:T(8,128)S(1)} %slice.62), channel_id=1, source_target_pairs={{1,0},{2,1},{3,2},{4,3},{5,4},{6,5},{7,6},{8,7},{9,8},{10,9},{11,1... | collective-permute-start | bytes 12296 | tf_op jit(solution)/shard_map/ppermute | solution.py:16
  6.6 1.1 constant_dynamic-update-slice_fusion.1
  7.9 0.8 pad_maximum_fusion.2
  8.7 4.5 %collective-permute-done = f32[64,16]{1,0:T(8,128)S(1)} collective-permute-done((f32[64,16]{1,0:T(8,128)S(1)}, f32[64,16]{1,0:T(8,128)S(1)}, u32[]{:S(2)}, u32[]{:S(2)}) %collective-permute-start) | collective-permute-done | bytes 4128 | tf_op jit(solution)/shard_map/ppermute | solution.py:16
  13.2 1.3 collective-permute-start.1
  14.7 4.3 %collective-permute-done.1 = f32[16,2064]{1,0:T(8,128)S(1)} collective-permute-done((f32[16,2064]{1,0:T(8,128)S(1)}, f32[16,2064]{1,0:T(8,128)S(1)}, u32[]{:S(2)}, u32[]{:S(2)}) %collective-permute-start.1) | collective-permute-done | bytes 132128 | tf_op jit(solution)/shard_map/ppermute | solution.py:16
  19.0 3.2 %reshape.132 = f32[5,16,129,16]{3,2,1,0:T(8,128)} reshape(f32[80,2064]{1,0:T(8,128)S(1)} %pad_maximum_fusion) | data formatting | bytes 1320960 | tf_op jit(solution)/shard_map/reshape | solution.py:43
  22.3 8.1 %fusion = f32[64,5,16,128]{3,0,2,1:T(8,128)S(1)} fusion(f32[16,64,1,1]{1,0,3,2:T(8,128)S(1)} %fusion.25, f32[5,16,129,16]{3,2,1,0:T(8,128)} %reshape.132), kind=kOutput, calls=%fused_computation | convolution fusion | flops 125829120 | bytes 7868416 | tf_op jit(solution)/shard_map/akbl,lp->akpb/dot_general | solution.py:47
  30.4 5.8 %add_bitcast_fusion = f32[5,16,64,128]{3,2,1,0:T(8,128)S(1)} fusion(f32[64,5,16,128]{3,0,2,1:T(8,128)S(1)} %fusion, f32[5,16,129,16]{3,2,1,0:T(8,128)S(1)} %copy-done, f32[32,32]{1,0:T(8,128)S(1)} %get-tuple-element.40, f32[32,32]{1,0:T(8,128)S(1)} %get-tuple-element.41), kind=kOutput, calls=%fused_computation.12 | convolution fusion | flops 126485504 | bytes 10518528 | tf_op jit(solution)/shard_map/akbl,lp->akpb/dot_general | solution.py:44
  36.2 0.6 fusion.35
  36.8 1.2 copy.29
  38.1 1.2 copy.30
  39.3 4.2 %fusion.4 = f32[4,32,128,64,1,1]{2,3,5,4,1,0:T(8,128)S(1)} fusion(f32[4,1,16,2,32,128]{5,2,3,1,4,0:T(8,128)S(1)} %copy.30, f32[4,1,16,2,32,128]{5,2,3,1,4,0:T(8,128)S(1)} %copy.29, f32[64,2,16,2]{0,2,3,1:T(8,128)S(1)} %maximum_maximum_fusion), kind=kOutput, calls=%fused_computation.4 | convolution fusion | flops 806354944 | bytes 8404992 | tf_op jit(solution)/shard_map/tm,amvb->atvb/dot_general | solution.py:54
  43.5 4.4 %fusion.11 = f32[4,64,32,128]{3,1,2,0:T(8,128)S(1)} fusion(f32[64,64,1,1]{0,1,3,2:T(8,128)S(1)} %bitcast.75, f32[4,32,128,64,1,1]{2,3,5,4,1,0:T(8,128)S(1)} %fusion.4, f32[4,128]{1,0:T(4,128)S(1)} %copy-done.4, f32[64,32]{0,1:T(8,128)S(1)} %copy.31), kind=kOutput, calls=%fused_computation.13 | convolution fusion | flops 807403520 | bytes 8415232 | tf_op jit(solution)/shard_map/tm,atvb->amvb/dot_general | solution.py:65
  47.9 2.4 %copy.33 = f32[4,64,32,128]{3,2,1,0:T(8,128)S(1)} copy(f32[4,64,32,128]{3,1,2,0:T(8,128)S(1)} %fusion.11) | data formatting | bytes 8388608 | tf_op jit(solution)/shard_map/tm,atvb->amvb/transpose | solution.py:65
  50.9 1.5 fusion.18
  52.4 1.5 fusion.19
  54.5 1.0 slice.74
  55.5 3.4 %collective-permute-start.2 = (f32[16,2064]{1,0:T(8,128)}, f32[16,2064]{1,0:T(8,128)}, u32[]{:S(2)}, u32[]{:S(2)}) collective-permute-start(f32[16,2064]{1,0:T(8,128)} %slice.74), channel_id=1, source_target_pairs={{0,64},{64,128},{128,192},{1,65},{65,129},{129,193},{2,66},{66,130... | collective-permute-start | bytes 396296 | tf_op jit(solution)/shard_map/ppermute | solution.py:16
  59.6 1.1 pad_add_fusion.3
  60.8 2.1 %copy.37 = f32[3,16,129,16]{3,2,1,0:T(8,128)S(1)} copy(f32[3,16,129,16]{2,3,1,0:T(8,128)} %pad_add_fusion.3) | data formatting | bytes 792576 | tf_op jit(solution)/shard_map/slice | solution.py:88
  62.9 1.6 slice.76
  64.5 1.0 add.58
  65.6 0.7 pad_maximum_fusion.1
  66.3 3.8 %collective-permute-start.3 = (f32[64,16]{1,0:T(8,128)S(1)}, f32[64,16]{1,0:T(8,128)S(1)}, u32[]{:S(2)}, u32[]{:S(2)}) collective-permute-start(f32[64,16]{1,0:T(8,128)S(1)} %pad_maximum_fusion.1), channel_id=1, source_target_pairs={{0,1},{1,2},{2,3},{3,4},{4,5},{5,6},{6,7},{7,8},{8,9},{9,10},{10,1... | collective-permute-start | bytes 12296 | tf_op jit(solution)/shard_map/ppermute | solution.py:16
  70.2 0.7 dynamic-slice
  71.1 0.7 maximum_add_fusion
  71.9 2.1 %multiply_reduce_fusion = (f32[]{:T(128)}, f32[]{:T(128)}, f32[]{:T(128)}, f32[]{:T(128)}, f32[64,2048]{1,0:T(8,128)S(1)}) fusion(f32[64,2048]{1,0:T(8,128)} %param.6, f32[64,2048]{1,0:T(8,128)} %param.7, f32[48,2064]{1,0:T(8,128)} %slice.76, f32[16,2064]{1,0:T(8,128)S(1)} %add.58, f32[64,16]{1,0:T(8,128)S(1)} %maximum_add_fusion), kind=kLoop, calls=%fused_computation.27 | loop fusion | flops 1966076 | bytes 2105360 | tf_op jit(solution)/shard_map/reduce_sum | solution.py:98
  74.0 1.4 dynamic-update-slice.10
  75.5 1.4 dynamic-update-slice.15
  76.9 1.4 dynamic-update-slice.5
  78.3 1.4 dynamic-update-slice
  80.3 6.7 %all-reduce.26 = (f32[4]{0:T(128)S(1)}, f32[4]{0:T(128)S(1)}, f32[4]{0:T(128)S(1)}, f32[4]{0:T(128)S(1)}) all-reduce(f32[4]{0:T(128)S(1)} %dynamic-update-slice, f32[4]{0:T(128)S(1)} %dynamic-update-slice.5, f32[4]{0:T(128)S(1)} %dynamic-update-slice.10, ...), channel_id=1, replica_groups=mesh['row'=4,'col_0'=4,'col_1'=4,'col_2'=2,'col_3'=2] {'row'}, use_global_device_ids=true, to_apply=%add.4 | all-reduce | flops 16 | bytes 128
  87.0 0.6 reduce_sum.229
  88.2 1.4 dynamic-update-slice.11
  89.6 1.4 dynamic-update-slice.16
  91.0 0.6 reduce_sum.223
  91.6 1.4 dynamic-update-slice.6
  93.0 0.6 reduce_sum.217
  93.6 1.4 dynamic-update-slice.1
  95.6 10.6 %all-reduce.25 = (f32[4]{0:T(128)S(1)}, f32[4]{0:T(128)S(1)}, f32[4]{0:T(128)S(1)}, f32[4]{0:T(128)S(1)}) all-reduce(f32[4]{0:T(128)S(1)} %dynamic-update-slice.1, f32[4]{0:T(128)S(1)} %dynamic-update-slice.6, f32[4]{0:T(128)S(1)} %dynamic-update-slice.11, ...), channel_id=1, replica_groups=mesh['row'=4,'col_0'=4,'col_1'=4,'col_2'=2,'col_3'=2] {'col_0'}, use_global_device_ids=true, to_apply=%add.5 | all-reduce | flops 16 | bytes 128
  106.2 0.6 reduce_sum.230
  107.4 1.4 dynamic-update-slice.12
  108.8 1.4 dynamic-update-slice.17
  110.8 1.4 dynamic-update-slice.7
  112.8 1.4 dynamic-update-slice.2
  114.8 7.8 %all-reduce.24 = (f32[4]{0:T(128)S(1)}, f32[4]{0:T(128)S(1)}, f32[4]{0:T(128)S(1)}, f32[4]{0:T(128)S(1)}) all-reduce(f32[4]{0:T(128)S(1)} %dynamic-update-slice.2, f32[4]{0:T(128)S(1)} %dynamic-update-slice.7, f32[4]{0:T(128)S(1)} %dynamic-update-slice.12, ...), channel_id=1, replica_groups=mesh['row'=4,'col_0'=4,'col_1'=4,'col_2'=2,'col_3'=2] {'col_1'}, use_global_device_ids=true, to_apply=%add.6 | all-reduce | flops 16 | bytes 128
  122.6 0.6 reduce_sum.231
  123.8 1.4 dynamic-update-slice.13
  125.2 1.4 dynamic-update-slice.18
  127.2 1.4 dynamic-update-slice.8
  129.2 1.4 dynamic-update-slice.3
  131.2 7.7 %all-reduce.28 = (f32[2]{0:T(128)S(1)}, f32[2]{0:T(128)S(1)}, f32[2]{0:T(128)S(1)}, f32[2]{0:T(128)S(1)}) all-reduce(f32[2]{0:T(128)S(1)} %dynamic-update-slice.3, f32[2]{0:T(128)S(1)} %dynamic-update-slice.8, f32[2]{0:T(128)S(1)} %dynamic-update-slice.13, ...), channel_id=1, replica_groups=mesh['row'=4,'col_0'=4,'col_1'=4,'col_2'=2,'col_3'=2] {'col_2'}, use_global_device_ids=true, to_apply=%add.7 | all-reduce | flops 8 | bytes 64
  138.9 0.6 reduce_sum.232
  140.1 1.4 dynamic-update-slice.14
  141.5 1.4 dynamic-update-slice.19
  143.5 1.4 dynamic-update-slice.9
  145.5 1.4 dynamic-update-slice.4
  146.9 16.7 %all-reduce.27 = (f32[2]{0:T(128)S(1)}, f32[2]{0:T(128)S(1)}, f32[2]{0:T(128)S(1)}, f32[2]{0:T(128)S(1)}) all-reduce(f32[2]{0:T(128)S(1)} %dynamic-update-slice.4, f32[2]{0:T(128)S(1)} %dynamic-update-slice.9, f32[2]{0:T(128)S(1)} %dynamic-update-slice.14, ...), channel_id=1, replica_groups=mesh['row'=4,'col_0'=4,'col_1'=4,'col_2'=2,'col_3'=2] {'col_3'}, use_global_device_ids=true, to_apply=%add.8 | all-reduce | flops 8 | bytes 64
  163.6 0.6 reduce_sum.221
  166.2 0.6 reduce_sum.233
  168.1 0.6 reduce_sum.239
  170.0 1.3 multiply_add_fusion
  (73 shorter events, 11.7 us)
Async XLA Ops:
  1.4 11.8 %collective-permute-start = (f32[64,16]{1,0:T(8,128)S(1)}, f32[64,16]{1,0:T(8,128)S(1)}, u32[]{:S(2)}, u32[]{:S(2)}) collective-permute-start(f32[64,16]{1,0:T(8,128)S(1)} %slice.62), channel_id=1, source_target_pairs={{1,0},{2,1},{3,2},{4,3},{5,4},{6,5},{7,6},{8,7},{9,8},{10,9},{11,1... | collective-permute-start | bytes 12296 | tf_op jit(solution)/shard_map/ppermute | solution.py:16
  13.2 5.8 %collective-permute-start.1 = (f32[16,2064]{1,0:T(8,128)S(1)}, f32[16,2064]{1,0:T(8,128)S(1)}, u32[]{:S(2)}, u32[]{:S(2)}) collective-permute-start(f32[16,2064]{1,0:T(8,128)S(1)} %slice.82), channel_id=1, source_target_pairs={{64,0},{128,64},{192,128},{65,1},{129,65},{193,129},{66,2},{130,66... | collective-permute-start | bytes 396296 | tf_op jit(solution)/shard_map/ppermute | solution.py:16
  22.3 8.1 %copy-start = (f32[5,16,129,16]{3,2,1,0:T(8,128)S(1)}, f32[5,16,129,16]{3,2,1,0:T(8,128)}, u32[]{:S(2)}) copy-start(f32[5,16,129,16]{3,2,1,0:T(8,128)} %reshape.132) | copy-start | bytes 1981444
  39.3 4.2 %copy-start.4 = (f32[4,128]{1,0:T(4,128)S(1)}, f32[4,128]{1,0:T(4,128)}, u32[]{:S(2)}) copy-start(f32[4,128]{1,0:T(4,128)} %param.8) | copy-start | bytes 6148
  55.5 9.0 %collective-permute-start.2 = (f32[16,2064]{1,0:T(8,128)}, f32[16,2064]{1,0:T(8,128)}, u32[]{:S(2)}, u32[]{:S(2)}) collective-permute-start(f32[16,2064]{1,0:T(8,128)} %slice.74), channel_id=1, source_target_pairs={{0,64},{64,128},{128,192},{1,65},{65,129},{129,193},{2,66},{66,130... | collective-permute-start | bytes 396296 | tf_op jit(solution)/shard_map/ppermute | solution.py:16
  62.9 7.3 %copy-start.9 = (u32[256]{0:T(256)S(1)}, u32[256]{0:T(256)}, u32[]{:S(2)}) copy-start(u32[256]{0:T(256)} %constant.40) | copy-start | bytes 3076
  64.5 15.2 %copy-start.8 = (u32[256]{0:T(256)S(1)}, u32[256]{0:T(256)}, u32[]{:S(2)}) copy-start(u32[256]{0:T(256)} %constant.45) | copy-start | bytes 3076
  64.5 30.5 %copy-start.7 = (u32[256]{0:T(256)S(1)}, u32[256]{0:T(256)}, u32[]{:S(2)}) copy-start(u32[256]{0:T(256)} %constant.50) | copy-start | bytes 3076
  64.5 49.7 %copy-start.6 = (u32[256]{0:T(256)S(1)}, u32[256]{0:T(256)}, u32[]{:S(2)}) copy-start(u32[256]{0:T(256)} %constant.55) | copy-start | bytes 3076
  64.5 66.1 %copy-start.5 = (u32[256]{0:T(256)S(1)}, u32[256]{0:T(256)}, u32[]{:S(2)}) copy-start(u32[256]{0:T(256)} %constant.60) | copy-start | bytes 3076
  64.5 105.5 %copy-start.1 = (f32[64,2048]{1,0:T(8,128)S(1)}, f32[64,2048]{1,0:T(8,128)}, u32[]{:S(2)}) copy-start(f32[64,2048]{1,0:T(8,128)} %param.7) | copy-start | bytes 1572868
  64.5 105.5 %copy-start.2 = (f32[64,2048]{1,0:T(8,128)S(1)}, f32[64,2048]{1,0:T(8,128)}, u32[]{:S(2)}) copy-start(f32[64,2048]{1,0:T(8,128)} %param.6) | copy-start | bytes 1572868
  64.5 105.5 %copy-start.3 = (f32[64,2048]{1,0:T(8,128)S(1)}, f32[64,2048]{1,0:T(8,128)}, u32[]{:S(2)}) copy-start(f32[64,2048]{1,0:T(8,128)} %param.5) | copy-start | bytes 1572868
  66.3 4.8 %collective-permute-start.3 = (f32[64,16]{1,0:T(8,128)S(1)}, f32[64,16]{1,0:T(8,128)S(1)}, u32[]{:S(2)}, u32[]{:S(2)}) collective-permute-start(f32[64,16]{1,0:T(8,128)S(1)} %pad_maximum_fusion.1), channel_id=1, source_target_pairs={{0,1},{1,2},{2,3},{3,4},{4,5},{5,6},{6,7},{7,8},{8,9},{9,10},{10,1... | collective-permute-start | bytes 12296 | tf_op jit(solution)/shard_map/ppermute | solution.py:16
